TPU v7x, 512 devices: a whole 4x4x16 slice. The times are simulated.
512 devices in a mesh: tok: 64 (over z, x), head: 8 (over y, core).
Axes of the slice: x: 4, y: 4, z: 16, core: 2. Of those that a mesh axis runs over, the one named last changes fastest.
Arguments:
- tokens: bfloat16 [32768, 2560], P('tok', 'head'), may hold values from -6 to 6
- query_weight: bfloat16 [2560, 2560], P('tok'), may hold values from -0.125 to 0.125
- keyvalue_weight: bfloat16 [2560, 512], P('tok'), may hold values from -0.125 to 0.125
- output_weight: bfloat16 [2560, 2560], P(None, ('head', 'tok')), may hold values from -0.125 to 0.125
- cache: bfloat16 [2048, 2, 128, 256], P(('tok', 'head')), may hold values from -460 to 460
- page_table: int32 [512, 4], P('tok'), may hold values from 0 to 2047, as said below
- parents: int32 [512, 64], P('tok'), may hold values from 0 to 62, as said below
- cache_len: int32 [512], P('tok'), may hold values from 1 to 448, as said below
- accepted_leaf: int32 [512], P('tok'), may hold values from 0 to 63
Outputs:
- attended: bfloat16 [32768, 2560], P('tok', 'head')
- cache_out: bfloat16 [2048, 2, 128, 256], P(('tok', 'head'))
Inputs may be any that keep to these rules, and one draw needn't show every extreme that they name: `page_table`: for every d, row d names each of the pages d * 4 to d * 4 + 3 exactly once, so request d's pages all lie on device d (devices counted tok-major, head-minor). parents[r, 0] = 0, and parents[r, i] < i for i >= 1. `cache_len`: roughly half of the requests hold at most 128 cached positions, the others more than 320.
All inputs are finite; a program needn't handle non-finite values.
Results may differ from a plain program's by a relative error of at most 0.014.
The roundings to bfloat16 on the way count: a program that leaves them out, or rounds other values in their place, can miss the bound.
Values may be sent and summed in bfloat16 or wider, within the bound.
No kernel may reach another device: no remote copies, remote signals or barrier semaphores. Data moves between devices by JAX's collectives and lax.ppermute only.
A program may use at most 64 MiB of HBM per device.

v0:
```python
import math
import jax
import jax.numpy as jnp
from jax import lax
from jax.sharding import Mesh, PartitionSpec as P

HQ = 10
HD = 256
DRAFT = 64
PAGE = 128
NPR = 4
WINDOW = 256


def ancestry(parent_row):
    node_ids = jnp.arange(DRAFT, dtype=jnp.int32)
    link = (parent_row[:, None] == node_ids[None, :]).astype(jnp.float32)
    reach = jnp.minimum(link + jnp.eye(DRAFT, dtype=jnp.float32), 1.0)
    for sweep in range((DRAFT - 1).bit_length()):
        reach = jnp.minimum(jnp.dot(reach, reach, precision=lax.Precision.HIGHEST), 1.0)
    depth = (jnp.sum(reach, axis=1) - 1.0).astype(jnp.int32)
    return (reach, depth)


def rotate(values, position):
    half = HD // 4
    freq = jnp.exp(jnp.arange(half, dtype=jnp.float32) * (-2.0 * math.log(10000.0) / (HD // 2)))
    angle = position.astype(jnp.float32)[..., None] * freq
    cosine = jnp.cos(angle)
    sine = jnp.sin(angle)
    first = values[..., :half]
    second = values[..., half : 2 * half]
    return jnp.concatenate(
        [first * cosine - second * sine, second * cosine + first * sine, values[..., 2 * half :]],
        axis=-1,
    )


def attend(queries, cache_keys, cache_values, tree_keys, tree_values, lengths, position, reach):
    window_span = cache_keys.shape[1]
    slot_ids = jnp.arange(window_span, dtype=jnp.int32)
    visible = (slot_ids[None, None, :] < lengths[:, None, None]) & (
        slot_ids[None, None, :] > position[:, :, None] - WINDOW
    )
    cache_scores = jnp.einsum(
        "rnhd,rcd->rhnc", queries, cache_keys, preferred_element_type=jnp.float32
    )
    tree_scores = jnp.einsum(
        "rnhd,rmd->rhnm", queries, tree_keys, preferred_element_type=jnp.float32
    )
    cache_scores = jnp.where(visible[:, None], cache_scores, -1e30)
    tree_scores = jnp.where(reach[:, None] > 0.5, tree_scores, -1e30)
    row_peak = jnp.maximum(jnp.max(cache_scores, axis=-1), jnp.max(tree_scores, axis=-1))[..., None]
    cache_weights = jnp.exp(cache_scores - row_peak)
    tree_weights = jnp.exp(tree_scores - row_peak)
    denominator = jnp.sum(cache_weights, axis=-1, keepdims=True) + jnp.sum(
        tree_weights, axis=-1, keepdims=True
    )
    cache_weights = (cache_weights / denominator).astype(jnp.bfloat16)
    tree_weights = (tree_weights / denominator).astype(jnp.bfloat16)
    result = jnp.einsum(
        "rhnc,rcd->rhnd", cache_weights, cache_values, preferred_element_type=jnp.float32
    )
    result = result + jnp.einsum(
        "rhnm,rmd->rhnd", tree_weights, tree_values, preferred_element_type=jnp.float32
    )
    return result.astype(jnp.bfloat16)


def refresh(logical_pages, length, leaf, reach, depth, new_keys, new_values):
    count = logical_pages.shape[0] * logical_pages.shape[2]
    logical = jnp.transpose(logical_pages, (1, 0, 2, 3)).reshape(2, count, HD)
    slot_ids = jnp.arange(count, dtype=jnp.int32)
    on_path = reach[leaf]
    selector = ((on_path[None, :] > 0.5) & (depth[None, :] == slot_ids[:, None] - length)).astype(
        jnp.float32
    )
    placed_keys = jnp.dot(selector, new_keys.astype(jnp.float32), precision=lax.Precision.HIGHEST)
    placed_values = jnp.dot(
        selector, new_values.astype(jnp.float32), precision=lax.Precision.HIGHEST
    )
    placed = jnp.stack([placed_keys, placed_values]).astype(jnp.bfloat16)
    written = jnp.sum(selector, axis=1) > 0.5
    logical = jnp.where(written[None, :, None], placed, logical)
    return jnp.transpose(
        logical.reshape(2, logical_pages.shape[0], logical_pages.shape[2], HD), (1, 0, 2, 3)
    )


def ring_pieces(piece, axis):
    size = lax.axis_size(axis)
    got = [(0, 0, piece)]
    ahead = piece
    behind = piece
    forward = [(i, (i + 1) % size) for i in range(size)]
    backward = [(i, (i - 1) % size) for i in range(size)]
    for step in range(1, size // 2 + 1):
        if 2 * step == size and size > 2:
            half = piece.shape[0] // 2
            got.append((step, 0, lax.ppermute(ahead[:half], axis, forward)))
            got.append((step, half, lax.ppermute(behind[half:], axis, backward)))
            break
        ahead = lax.ppermute(ahead, axis, forward)
        got.append((size - step, 0, ahead))
        if step <= (size - 1) // 2:
            behind = lax.ppermute(behind, axis, backward)
            got.append((step, 0, behind))
    return got


def grid_gather(piece):
    z_size = lax.axis_size("tz")
    x_size = lax.axis_size("tx")
    z_index = lax.axis_index("tz")
    x_index = lax.axis_index("tx")
    zero = jnp.int32(0)
    column = jnp.zeros((z_size,) + piece.shape, piece.dtype)
    for offset, first, part in ring_pieces(piece, "tz"):
        column = lax.dynamic_update_slice(
            column, part[None], ((z_index + offset) % z_size, jnp.int32(first), zero)
        )
    placed = jnp.zeros((z_size, x_size) + piece.shape, piece.dtype)
    for offset, first, part in ring_pieces(column, "tx"):
        placed = lax.dynamic_update_slice(
            placed, part[:, None], (jnp.int32(first), (x_index + offset) % x_size, zero, zero)
        )
    return placed.reshape((z_size * x_size,) + piece.shape)


def shards(
    tokens,
    query_weight,
    keyvalue_weight,
    output_weight,
    cache,
    page_table,
    parents,
    cache_len,
    accepted_leaf,
):
    head_count = lax.axis_size("head")
    head_index = lax.axis_index("head")
    tok_index = lax.axis_index("tz") * lax.axis_size("tx") + lax.axis_index("tx")
    requests = parents.shape[0]
    assert requests == head_count
    pages_dev = cache.shape[0]
    part_rows = query_weight.shape[0]
    q_cols = HQ * HD // head_count
    kv_cols = 2 * HD // head_count
    out_cols = output_weight.shape[1]
    wq_piece = lax.dynamic_slice_in_dim(query_weight, head_index * q_cols, q_cols, axis=1)
    wkv_piece = lax.dynamic_slice_in_dim(keyvalue_weight, head_index * kv_cols, kv_cols, axis=1)
    proj_piece = jnp.concatenate([wq_piece, wkv_piece], axis=1)
    width = proj_piece.shape[1]
    wo_flat = output_weight.reshape(-1)
    wo_rows = -(-wo_flat.shape[0] // width)
    wo_rows = -(-(part_rows + wo_rows) // 8) * 8 - part_rows
    wo_block = jnp.pad(wo_flat, (0, wo_rows * width - wo_flat.shape[0])).reshape(wo_rows, width)
    piece = jnp.concatenate([proj_piece, wo_block], axis=0)
    stacked = grid_gather(piece)
    tok_count = stacked.shape[0]
    proj_w = stacked[:, :part_rows].reshape(tok_count * part_rows, width)
    wo_cols = (
        stacked[:, part_rows:]
        .reshape(tok_count, -1)[:, : wo_flat.shape[0]]
        .reshape(tok_count, HQ * HD, out_cols)
        .transpose(1, 0, 2)
        .reshape(HQ * HD, tok_count * out_cols)
    )
    gathered = lax.all_gather(tokens, "head", axis=1, tiled=True)
    wide = gathered.astype(jnp.float32)
    mean_square = jnp.mean(wide * wide, axis=1, keepdims=True)
    normed = (wide * lax.rsqrt(mean_square + 1e-06)).astype(jnp.bfloat16)
    both = jnp.dot(normed, proj_w, preferred_element_type=jnp.float32)
    mine = lax.all_to_all(both, "head", 0, 1, tiled=True)
    mine = mine.reshape(DRAFT, head_count, q_cols + kv_cols)
    q_pre = mine[:, :, :q_cols].reshape(DRAFT, HQ, HD)
    kv_pre = mine[:, :, q_cols:].reshape(DRAFT, 2 * HD)
    parent_row = lax.dynamic_index_in_dim(parents, head_index, 0, keepdims=False)
    length = lax.dynamic_index_in_dim(cache_len, head_index, 0, keepdims=False)
    leaf = lax.dynamic_index_in_dim(accepted_leaf, head_index, 0, keepdims=False)
    reach, depth = ancestry(parent_row)
    position = length + depth
    queries = (rotate(q_pre, position[:, None]) * HD ** (-0.5)).astype(jnp.bfloat16)
    tree_keys = rotate(kv_pre[:, :HD], position).astype(jnp.bfloat16)
    tree_values = kv_pre[:, HD:].astype(jnp.bfloat16)
    device = tok_index * head_count + head_index
    own_table = (
        lax.dynamic_index_in_dim(page_table, head_index, 0, keepdims=False) - device * pages_dev
    )
    own_pages = jnp.take(cache, own_table, axis=0)
    cache_keys = own_pages[:, 0].reshape(NPR * PAGE, HD)
    cache_values = own_pages[:, 1].reshape(NPR * PAGE, HD)
    result = attend(
        queries[None],
        cache_keys[None],
        cache_values[None],
        tree_keys[None],
        tree_values[None],
        length[None],
        position[None],
        reach[None],
    )
    mixed = lax.all_gather(result[0], "head", axis=1, tiled=True)
    per_head = lax.dot_general(
        mixed,
        wo_cols.reshape(HQ, HD, wo_cols.shape[1]),
        (((2,), (1,)), ((0,), (0,))),
        preferred_element_type=jnp.float32,
    )
    summed = None
    for group in range(head_count):
        head_ids = [k for k in range(group, HQ, head_count)]
        if not head_ids:
            continue
        partial_value = per_head[head_ids[0]]
        for k in head_ids[1:]:
            partial_value = partial_value + per_head[k]
        term = partial_value.astype(jnp.bfloat16).astype(jnp.float32)
        summed = term if summed is None else summed + term
    attended = summed.astype(jnp.bfloat16)
    new_pages = refresh(own_pages, length, leaf, reach, depth, tree_keys, tree_values)
    matches = (own_table[:, None] == jnp.arange(pages_dev, dtype=jnp.int32)[None, :]).astype(
        jnp.int32
    )
    inverse = jnp.sum(matches * jnp.arange(pages_dev, dtype=jnp.int32)[:, None], axis=0)
    cache_out = jnp.take(new_pages, inverse, axis=0)
    return (attended, cache_out)


def solution(mesh):
    tok_size = mesh.shape["tok"]
    tx_size = 4 if tok_size % 4 == 0 else tok_size
    grid = Mesh(
        mesh.devices.reshape(tok_size // tx_size, tx_size, mesh.shape["head"]), ("tz", "tx", "head")
    )
    tok = ("tz", "tx")
    in_specs = (
        P(tok, "head"),
        P(tok, None),
        P(tok, None),
        P(None, ("head",) + tok),
        P(tok + ("head",), None, None, None),
        P(tok, None),
        P(tok, None),
        P(tok),
        P(tok),
    )
    out_specs = (P(tok, "head"), P(tok + ("head",), None, None, None))
    return jax.shard_map(shards, mesh=grid, in_specs=in_specs, out_specs=out_specs, check_vma=False)
```

profile of v0, /device:TPU:1, one launch (start us, length us, event | category | flops | bytes accessed | tf_op | source)
XLA Modules:
  0.0 198.7 jit_solution(2662571134446232722)
XLA Ops:
  7.3 1.2 copy.43
  8.5 1.0 reshape.344
  9.5 0.8 constant_dynamic-slice_fusion.1
  10.3 0.9 constant_dynamic-slice_fusion.2
  11.3 4.4 %collective-permute-start = (bf16[80,384]{1,0:T(8,128)(2,1)S(1)}, bf16[80,384]{1,0:T(8,128)(2,1)S(1)}, u32[]{:S(2)}, u32[]{:S(2)}) collective-permute-start(bf16[80,384]{1,0:T(8,128)(2,1)S(1)} %get-tuple-element.6), channel_id=1, source_target_pairs={{0,32},{32,64},{64,96},{96,128},{128,160},{160,192},{192,224},{224... | collective-permute-start | bytes 184328 | tf_op jit(solution)/shard_map/ppermute | solution.py:103
  15.7 9.5 %collective-permute-start.1 = (bf16[80,384]{1,0:T(8,128)(2,1)S(1)}, bf16[80,384]{1,0:T(8,128)(2,1)S(1)}, u32[]{:S(2)}, u32[]{:S(2)}) collective-permute-start(bf16[80,384]{1,0:T(8,128)(2,1)S(1)} %get-tuple-element.6), channel_id=1, source_target_pairs={{0,480},{32,0},{64,32},{96,64},{128,96},{160,128},{192,160},{224,1... | collective-permute-start | bytes 184328 | tf_op jit(solution)/shard_map/ppermute | solution.py:106
  27.9 0.7 fusion.38
  31.4 0.7 iota_compare_fusion.6
  32.1 1.9 collective-permute-start.2
  34.0 4.6 %collective-permute-start.3 = (bf16[80,384]{1,0:T(8,128)(2,1)S(1)}, bf16[80,384]{1,0:T(8,128)(2,1)S(1)}, u32[]{:S(2)}, u32[]{:S(2)}) collective-permute-start(bf16[80,384]{1,0:T(8,128)(2,1)S(1)} %collective-permute-done.1), channel_id=1, source_target_pairs={{0,480},{32,0},{64,32},{96,64},{128,96},{160,128},{192,160},{224,1... | collective-permute-start | bytes 184328 | tf_op jit(solution)/shard_map/ppermute | solution.py:106
  38.6 1.9 collective-permute-start.4
  40.6 4.6 %collective-permute-start.5 = (bf16[80,384]{1,0:T(8,128)(2,1)S(1)}, bf16[80,384]{1,0:T(8,128)(2,1)S(1)}, u32[]{:S(2)}, u32[]{:S(2)}) collective-permute-start(bf16[80,384]{1,0:T(8,128)(2,1)S(1)} %collective-permute-done.3), channel_id=1, source_target_pairs={{0,480},{32,0},{64,32},{96,64},{128,96},{160,128},{192,160},{224,1... | collective-permute-start | bytes 184328 | tf_op jit(solution)/shard_map/ppermute | solution.py:106
  45.2 1.9 collective-permute-start.6
  47.2 4.6 %collective-permute-start.7 = (bf16[80,384]{1,0:T(8,128)(2,1)S(1)}, bf16[80,384]{1,0:T(8,128)(2,1)S(1)}, u32[]{:S(2)}, u32[]{:S(2)}) collective-permute-start(bf16[80,384]{1,0:T(8,128)(2,1)S(1)} %collective-permute-done.5), channel_id=1, source_target_pairs={{0,480},{32,0},{64,32},{96,64},{128,96},{160,128},{192,160},{224,1... | collective-permute-start | bytes 184328 | tf_op jit(solution)/shard_map/ppermute | solution.py:106
  51.8 1.9 collective-permute-start.8
  53.7 4.6 %collective-permute-start.9 = (bf16[80,384]{1,0:T(8,128)(2,1)S(1)}, bf16[80,384]{1,0:T(8,128)(2,1)S(1)}, u32[]{:S(2)}, u32[]{:S(2)}) collective-permute-start(bf16[80,384]{1,0:T(8,128)(2,1)S(1)} %collective-permute-done.7), channel_id=1, source_target_pairs={{0,480},{32,0},{64,32},{96,64},{128,96},{160,128},{192,160},{224,1... | collective-permute-start | bytes 184328 | tf_op jit(solution)/shard_map/ppermute | solution.py:106
  58.4 1.9 collective-permute-start.10
  60.3 4.6 %collective-permute-start.11 = (bf16[80,384]{1,0:T(8,128)(2,1)S(1)}, bf16[80,384]{1,0:T(8,128)(2,1)S(1)}, u32[]{:S(2)}, u32[]{:S(2)}) collective-permute-start(bf16[80,384]{1,0:T(8,128)(2,1)S(1)} %collective-permute-done.9), channel_id=1, source_target_pairs={{0,480},{32,0},{64,32},{96,64},{128,96},{160,128},{192,160},{224,1... | collective-permute-start | bytes 184328 | tf_op jit(solution)/shard_map/ppermute | solution.py:106
  65.0 1.9 collective-permute-start.12
  66.9 4.6 %collective-permute-start.13 = (bf16[80,384]{1,0:T(8,128)(2,1)S(1)}, bf16[80,384]{1,0:T(8,128)(2,1)S(1)}, u32[]{:S(2)}, u32[]{:S(2)}) collective-permute-start(bf16[80,384]{1,0:T(8,128)(2,1)S(1)} %collective-permute-done.11), channel_id=1, source_target_pairs={{0,480},{32,0},{64,32},{96,64},{128,96},{160,128},{192,160},{224,1... | collective-permute-start | bytes 184328 | tf_op jit(solution)/shard_map/ppermute | solution.py:106
  71.6 1.9 collective-permute-start.14
  73.5 4.6 %collective-permute-start.15 = (bf16[40,384]{1,0:T(8,128)(2,1)S(1)}, bf16[40,384]{1,0:T(8,128)(2,1)S(1)}, u32[]{:S(2)}, u32[]{:S(2)}) collective-permute-start(bf16[40,384]{1,0:T(8,128)(2,1)S(1)} %slice.130), channel_id=1, source_target_pairs={{0,480},{32,0},{64,32},{96,64},{128,96},{160,128},{192,160},{224,1... | collective-permute-start | bytes 92168 | tf_op jit(solution)/shard_map/ppermute | solution.py:101
  78.2 0.9 collective-permute-done.15
  79.1 4.4 %collective-permute-start.17 = (bf16[16,80,384]{2,1,0:T(8,128)(2,1)S(1)}, bf16[16,80,384]{2,1,0:T(8,128)(2,1)S(1)}, u32[]{:S(2)}, u32[]{:S(2)}) collective-permute-start(bf16[16,80,384]{2,1,0:T(8,128)(2,1)S(1)} %bitcast_dynamic-update-slice_fusion.20), channel_id=1, source_target_pairs={{0,24},{8,0},{16,8},{24,16},{1,25},{9,1},{17,9},{25,17},{2,26},{10... | collective-permute-start | bytes 2949128 | tf_op jit(solution)/shard_map/ppermute | solution.py:106
  83.5 1.9 collective-permute-start.16
  86.5 11.6 %collective-permute-done.17 = bf16[16,80,384]{2,1,0:T(8,128)(2,1)S(1)} collective-permute-done((bf16[16,80,384]{2,1,0:T(8,128)(2,1)S(1)}, bf16[16,80,384]{2,1,0:T(8,128)(2,1)S(1)}, u32[]{:S(2)}, u32[]{:S(2)}) %collective-permute-start.17) | collective-permute-done | bytes 983072 | tf_op jit(solution)/shard_map/ppermute | solution.py:106
  98.1 5.3 %collective-permute-start.19 = (bf16[8,80,384]{2,1,0:T(8,128)(2,1)S(1)}, bf16[8,80,384]{2,1,0:T(8,128)(2,1)S(1)}, u32[]{:S(2)}, u32[]{:S(2)}) collective-permute-start(bf16[8,80,384]{2,1,0:T(8,128)(2,1)S(1)} %slice.132), channel_id=1, source_target_pairs={{0,24},{8,0},{16,8},{24,16},{1,25},{9,1},{17,9},{25,17},{2,26},{10... | collective-permute-start | bytes 1474568 | tf_op jit(solution)/shard_map/ppermute | solution.py:101
  103.5 1.9 collective-permute-start.18
  105.9 9.5 %collective-permute-done.18 = bf16[8,80,384]{2,1,0:T(8,128)(2,1)S(1)} collective-permute-done((bf16[8,80,384]{2,1,0:T(8,128)(2,1)S(1)}, bf16[8,80,384]{2,1,0:T(8,128)(2,1)S(1)}, u32[]{:S(2)}, u32[]{:S(2)}) %collective-permute-start.18) | collective-permute-done | bytes 491552 | tf_op jit(solution)/shard_map/ppermute | solution.py:100
  115.5 2.3 %fusion.44 = (bf16[64,40,384]{2,1,0:T(8,128)(2,1)}, bf16[64,40,384]{2,1,0:T(8,128)(2,1)}) fusion(bf16[64,80,384]{2,1,0:T(8,128)(2,1)S(1)} %bitcast.125), kind=kLoop, calls=%fused_computation.126 | loop fusion | bytes 7864320 | tf_op jit(solution)/shard_map/slice | solution.py:164
  117.8 3.0 %copy.42 = bf16[512,2560]{1,0:T(8,128)(2,1)S(1)} copy(bf16[512,2560]{0,1:T(8,128)(2,1)} %all-gather.3.cloned.1.call-done) | data formatting | bytes 5242880 | tf_op jit(solution)/shard_map/all_gather | solution.py:170
  121.9 1.0 copy-done.3
  123.0 2.4 %fusion.50 = f32[8,64,384]{2,1,0:T(8,128)} fusion(bf16[8,64,2560]{2,1,0:T(8,128)(2,1)S(1)} %bitcast.129, bf16[2560,384,1]{1,0,2:T(8,128)(2,1)S(1)} %bitcast.130), kind=kOutput, calls=%fused_computation.132 | convolution fusion | flops 1006632960 | bytes 5373952 | tf_op jit(solution)/shard_map/dot_general | solution.py:174
  125.4 13.3 %all-to-all-start = ((f32[8,64,384]{2,1,0:T(8,128)}), f32[8,64,384]{2,1,0:T(8,128)S(1)}, u32[]{:S(2)}, u32[]{:S(2)}) async-start(f32[8,64,384]{2,1,0:T(8,128)} %fusion.50), calls=%async_computation | async-start | bytes 1572864 | tf_op jit(solution)/shard_map/all_to_all | solution.py:175
  139.4 0.7 add_add_fusion
  140.2 10.7 %all-to-all-done = f32[8,64,384]{2,1,0:T(8,128)S(1)} async-done(((f32[8,64,384]{2,1,0:T(8,128)}), f32[8,64,384]{2,1,0:T(8,128)S(1)}, u32[]{:S(2)}, u32[]{:S(2)}) %all-to-all-start) | async-done | bytes 786464 | tf_op jit(solution)/shard_map/all_to_all | solution.py:175
  153.3 1.0 fusion.13
  156.4 1.2 fusion.5
  158.0 3.8 %copy.51 = bf16[64,40,384]{0,2,1:T(8,128)(2,1)} copy(bf16[64,40,384]{2,1,0:T(8,128)(2,1)S(1)} %copy-done.2) | data formatting | bytes 3932160 | tf_op jit(solution)/shard_map/slice | solution.py:164
  161.8 3.3 %slice.145 = bf16[64,12800]{0,1:T(8,128)(2,1)} slice(bf16[64,15360]{0,1:T(8,128)(2,1)} %bitcast.126), slice={[0:64], [0:12800]} | slice | bytes 3276800 | tf_op jit(solution)/shard_map/slice | solution.py:164
  165.1 7.1 %reshape.354 = bf16[64,2560,5]{0,2,1:T(8,128)(2,1)} reshape(bf16[64,12800]{0,1:T(8,128)(2,1)} %slice.145) | data formatting | bytes 3276800 | tf_op jit(solution)/shard_map/reshape | solution.py:166
  172.2 7.0 %copy.52 = bf16[2560,64,5]{0,2,1:T(8,128)(2,1)S(1)} copy(bf16[2560,64,5]{1,2,0:T(8,128)(2,1)} %bitcast.124) | data formatting | bytes 3276800 | tf_op jit(solution)/shard_map/transpose | solution.py:167
  179.3 3.1 %reshape_reshape.3 = bf16[10,256,320]{1,0,2:T(8,128)(2,1)} reshape(bf16[2560,64,5]{0,2,1:T(8,128)(2,1)S(1)} %copy.52) | data formatting | bytes 3276800 | tf_op jit(solution)/shard_map/reshape;reshape | solution.py:207
  182.3 1.6 gather_fusion.1
  184.0 0.9 broadcast_select_fusion
  184.9 1.8 all-gather.5.cloned.1.call-done
  186.7 4.0 %fusion.49 = (bf16[10,512,320]{1,2,0:T(8,128)(2,1)S(1)}, f32[10,512,320]{1,2,0:T(8,128)S(1)}) fusion(bf16[10,512,256]{2,1,0:T(8,128)(2,1)} %all-gather.5.cloned.1.call-done, bf16[10,256,320]{1,0,2:T(8,128)(2,1)} %reshape_reshape.3), kind=kOutput, calls=%fused_computation.131 | convolution fusion | flops 840499200 | bytes 14090240 | tf_op jit(solution)/shard_map/dot_general | solution.py:205
  190.7 1.2 fusion.14
  (115 shorter events, 12.2 us)
Async XLA Ops:
  7.2 131.6 %copy-start = (bf16[4,2,128,256]{3,2,1,0:T(8,128)(2,1)S(1)}, bf16[4,2,128,256]{3,2,1,0:T(8,128)(2,1)}, u32[]{:S(2)}) copy-start(bf16[4,2,128,256]{3,2,1,0:T(8,128)(2,1)} %param.15) | copy-start | bytes 1572868
  7.2 18.2 %copy-start.5 = (s32[8]{0:T(128)S(1)}, s32[8]{0:T(128)}, u32[]{:S(2)}) copy-start(s32[8]{0:T(128)} %param.19) | copy-start | bytes 100
  7.2 20.1 %copy-start.6 = (s32[8]{0:T(128)S(1)}, s32[8]{0:T(128)}, u32[]{:S(2)}) copy-start(s32[8]{0:T(128)} %param.18) | copy-start | bytes 100
  7.2 21.4 %copy-start.4 = (s32[8,4]{0,1:T(4,128)S(1)}, s32[8,4]{0,1:T(4,128)}, u32[]{:S(2)}) copy-start(s32[8,4]{0,1:T(4,128)} %param.16) | copy-start | bytes 388
  7.2 110.6 %all-gather.3.cloned.1.call-start = ((), (), s32[]{:S(2)}) async-start(), calls=%async_computation.1 | async-start | bytes 2949120 | tf_op jit(solution)/shard_map/all_gather | solution.py:170
  11.3 20.7 %collective-permute-start = (bf16[80,384]{1,0:T(8,128)(2,1)S(1)}, bf16[80,384]{1,0:T(8,128)(2,1)S(1)}, u32[]{:S(2)}, u32[]{:S(2)}) collective-permute-start(bf16[80,384]{1,0:T(8,128)(2,1)S(1)} %get-tuple-element.6), channel_id=1, source_target_pairs={{0,32},{32,64},{64,96},{96,128},{128,160},{160,192},{192,224},{224... | collective-permute-start | bytes 184328 | tf_op jit(solution)/shard_map/ppermute | solution.py:103
  15.7 18.3 %collective-permute-start.1 = (bf16[80,384]{1,0:T(8,128)(2,1)S(1)}, bf16[80,384]{1,0:T(8,128)(2,1)S(1)}, u32[]{:S(2)}, u32[]{:S(2)}) collective-permute-start(bf16[80,384]{1,0:T(8,128)(2,1)S(1)} %get-tuple-element.6), channel_id=1, source_target_pairs={{0,480},{32,0},{64,32},{96,64},{128,96},{160,128},{192,160},{224,1... | collective-permute-start | bytes 184328 | tf_op jit(solution)/shard_map/ppermute | solution.py:106
  32.1 6.6 %collective-permute-start.2 = (bf16[80,384]{1,0:T(8,128)(2,1)S(1)}, bf16[80,384]{1,0:T(8,128)(2,1)S(1)}, u32[]{:S(2)}, u32[]{:S(2)}) collective-permute-start(bf16[80,384]{1,0:T(8,128)(2,1)S(1)} %collective-permute-done), channel_id=1, source_target_pairs={{0,32},{32,64},{64,96},{96,128},{128,160},{160,192},{192,224},{224... | collective-permute-start | bytes 184328 | tf_op jit(solution)/shard_map/ppermute | solution.py:103
  34.0 6.6 %collective-permute-start.3 = (bf16[80,384]{1,0:T(8,128)(2,1)S(1)}, bf16[80,384]{1,0:T(8,128)(2,1)S(1)}, u32[]{:S(2)}, u32[]{:S(2)}) collective-permute-start(bf16[80,384]{1,0:T(8,128)(2,1)S(1)} %collective-permute-done.1), channel_id=1, source_target_pairs={{0,480},{32,0},{64,32},{96,64},{128,96},{160,128},{192,160},{224,1... | collective-permute-start | bytes 184328 | tf_op jit(solution)/shard_map/ppermute | solution.py:106
  38.6 6.6 %collective-permute-start.4 = (bf16[80,384]{1,0:T(8,128)(2,1)S(1)}, bf16[80,384]{1,0:T(8,128)(2,1)S(1)}, u32[]{:S(2)}, u32[]{:S(2)}) collective-permute-start(bf16[80,384]{1,0:T(8,128)(2,1)S(1)} %collective-permute-done.2), channel_id=1, source_target_pairs={{0,32},{32,64},{64,96},{96,128},{128,160},{160,192},{192,224},{224... | collective-permute-start | bytes 184328 | tf_op jit(solution)/shard_map/ppermute | solution.py:103
  40.6 6.6 %collective-permute-start.5 = (bf16[80,384]{1,0:T(8,128)(2,1)S(1)}, bf16[80,384]{1,0:T(8,128)(2,1)S(1)}, u32[]{:S(2)}, u32[]{:S(2)}) collective-permute-start(bf16[80,384]{1,0:T(8,128)(2,1)S(1)} %collective-permute-done.3), channel_id=1, source_target_pairs={{0,480},{32,0},{64,32},{96,64},{128,96},{160,128},{192,160},{224,1... | collective-permute-start | bytes 184328 | tf_op jit(solution)/shard_map/ppermute | solution.py:106
  45.2 6.6 %collective-permute-start.6 = (bf16[80,384]{1,0:T(8,128)(2,1)S(1)}, bf16[80,384]{1,0:T(8,128)(2,1)S(1)}, u32[]{:S(2)}, u32[]{:S(2)}) collective-permute-start(bf16[80,384]{1,0:T(8,128)(2,1)S(1)} %collective-permute-done.4), channel_id=1, source_target_pairs={{0,32},{32,64},{64,96},{96,128},{128,160},{160,192},{192,224},{224... | collective-permute-start | bytes 184328 | tf_op jit(solution)/shard_map/ppermute | solution.py:103
  47.2 6.6 %collective-permute-start.7 = (bf16[80,384]{1,0:T(8,128)(2,1)S(1)}, bf16[80,384]{1,0:T(8,128)(2,1)S(1)}, u32[]{:S(2)}, u32[]{:S(2)}) collective-permute-start(bf16[80,384]{1,0:T(8,128)(2,1)S(1)} %collective-permute-done.5), channel_id=1, source_target_pairs={{0,480},{32,0},{64,32},{96,64},{128,96},{160,128},{192,160},{224,1... | collective-permute-start | bytes 184328 | tf_op jit(solution)/shard_map/ppermute | solution.py:106
  51.8 6.6 %collective-permute-start.8 = (bf16[80,384]{1,0:T(8,128)(2,1)S(1)}, bf16[80,384]{1,0:T(8,128)(2,1)S(1)}, u32[]{:S(2)}, u32[]{:S(2)}) collective-permute-start(bf16[80,384]{1,0:T(8,128)(2,1)S(1)} %collective-permute-done.6), channel_id=1, source_target_pairs={{0,32},{32,64},{64,96},{96,128},{128,160},{160,192},{192,224},{224... | collective-permute-start | bytes 184328 | tf_op jit(solution)/shard_map/ppermute | solution.py:103
  53.7 6.6 %collective-permute-start.9 = (bf16[80,384]{1,0:T(8,128)(2,1)S(1)}, bf16[80,384]{1,0:T(8,128)(2,1)S(1)}, u32[]{:S(2)}, u32[]{:S(2)}) collective-permute-start(bf16[80,384]{1,0:T(8,128)(2,1)S(1)} %collective-permute-done.7), channel_id=1, source_target_pairs={{0,480},{32,0},{64,32},{96,64},{128,96},{160,128},{192,160},{224,1... | collective-permute-start | bytes 184328 | tf_op jit(solution)/shard_map/ppermute | solution.py:106
  58.4 6.6 %collective-permute-start.10 = (bf16[80,384]{1,0:T(8,128)(2,1)S(1)}, bf16[80,384]{1,0:T(8,128)(2,1)S(1)}, u32[]{:S(2)}, u32[]{:S(2)}) collective-permute-start(bf16[80,384]{1,0:T(8,128)(2,1)S(1)} %collective-permute-done.8), channel_id=1, source_target_pairs={{0,32},{32,64},{64,96},{96,128},{128,160},{160,192},{192,224},{224... | collective-permute-start | bytes 184328 | tf_op jit(solution)/shard_map/ppermute | solution.py:103
  60.3 6.6 %collective-permute-start.11 = (bf16[80,384]{1,0:T(8,128)(2,1)S(1)}, bf16[80,384]{1,0:T(8,128)(2,1)S(1)}, u32[]{:S(2)}, u32[]{:S(2)}) collective-permute-start(bf16[80,384]{1,0:T(8,128)(2,1)S(1)} %collective-permute-done.9), channel_id=1, source_target_pairs={{0,480},{32,0},{64,32},{96,64},{128,96},{160,128},{192,160},{224,1... | collective-permute-start | bytes 184328 | tf_op jit(solution)/shard_map/ppermute | solution.py:106
  65.0 6.6 %collective-permute-start.12 = (bf16[80,384]{1,0:T(8,128)(2,1)S(1)}, bf16[80,384]{1,0:T(8,128)(2,1)S(1)}, u32[]{:S(2)}, u32[]{:S(2)}) collective-permute-start(bf16[80,384]{1,0:T(8,128)(2,1)S(1)} %collective-permute-done.10), channel_id=1, source_target_pairs={{0,32},{32,64},{64,96},{96,128},{128,160},{160,192},{192,224},{224... | collective-permute-start | bytes 184328 | tf_op jit(solution)/shard_map/ppermute | solution.py:103
  66.9 6.6 %collective-permute-start.13 = (bf16[80,384]{1,0:T(8,128)(2,1)S(1)}, bf16[80,384]{1,0:T(8,128)(2,1)S(1)}, u32[]{:S(2)}, u32[]{:S(2)}) collective-permute-start(bf16[80,384]{1,0:T(8,128)(2,1)S(1)} %collective-permute-done.11), channel_id=1, source_target_pairs={{0,480},{32,0},{64,32},{96,64},{128,96},{160,128},{192,160},{224,1... | collective-permute-start | bytes 184328 | tf_op jit(solution)/shard_map/ppermute | solution.py:106
  71.6 6.6 %collective-permute-start.14 = (bf16[40,384]{1,0:T(8,128)(2,1)S(1)}, bf16[40,384]{1,0:T(8,128)(2,1)S(1)}, u32[]{:S(2)}, u32[]{:S(2)}) collective-permute-start(bf16[40,384]{1,0:T(8,128)(2,1)S(1)} %slice.129), channel_id=1, source_target_pairs={{0,32},{32,64},{64,96},{96,128},{128,160},{160,192},{192,224},{224... | collective-permute-start | bytes 92168 | tf_op jit(solution)/shard_map/ppermute | solution.py:100
  73.5 5.6 %collective-permute-start.15 = (bf16[40,384]{1,0:T(8,128)(2,1)S(1)}, bf16[40,384]{1,0:T(8,128)(2,1)S(1)}, u32[]{:S(2)}, u32[]{:S(2)}) collective-permute-start(bf16[40,384]{1,0:T(8,128)(2,1)S(1)} %slice.130), channel_id=1, source_target_pairs={{0,480},{32,0},{64,32},{96,64},{128,96},{160,128},{192,160},{224,1... | collective-permute-start | bytes 92168 | tf_op jit(solution)/shard_map/ppermute | solution.py:101
  79.1 19.0 %collective-permute-start.17 = (bf16[16,80,384]{2,1,0:T(8,128)(2,1)S(1)}, bf16[16,80,384]{2,1,0:T(8,128)(2,1)S(1)}, u32[]{:S(2)}, u32[]{:S(2)}) collective-permute-start(bf16[16,80,384]{2,1,0:T(8,128)(2,1)S(1)} %bitcast_dynamic-update-slice_fusion.20), channel_id=1, source_target_pairs={{0,24},{8,0},{16,8},{24,16},{1,25},{9,1},{17,9},{25,17},{2,26},{10... | collective-permute-start | bytes 2949128 | tf_op jit(solution)/shard_map/ppermute | solution.py:106
  83.5 20.0 %collective-permute-start.16 = (bf16[16,80,384]{2,1,0:T(8,128)(2,1)S(1)}, bf16[16,80,384]{2,1,0:T(8,128)(2,1)S(1)}, u32[]{:S(2)}, u32[]{:S(2)}) collective-permute-start(bf16[16,80,384]{2,1,0:T(8,128)(2,1)S(1)} %bitcast_dynamic-update-slice_fusion.20), channel_id=1, source_target_pairs={{0,8},{8,16},{16,24},{24,0},{1,9},{9,17},{17,25},{25,1},{2,10},{10... | collective-permute-start | bytes 2949128 | tf_op jit(solution)/shard_map/ppermute | solution.py:103
  98.1 17.3 %collective-permute-start.19 = (bf16[8,80,384]{2,1,0:T(8,128)(2,1)S(1)}, bf16[8,80,384]{2,1,0:T(8,128)(2,1)S(1)}, u32[]{:S(2)}, u32[]{:S(2)}) collective-permute-start(bf16[8,80,384]{2,1,0:T(8,128)(2,1)S(1)} %slice.132), channel_id=1, source_target_pairs={{0,24},{8,0},{16,8},{24,16},{1,25},{9,1},{17,9},{25,17},{2,26},{10... | collective-permute-start | bytes 1474568 | tf_op jit(solution)/shard_map/ppermute | solution.py:101
  103.5 11.8 %collective-permute-start.18 = (bf16[8,80,384]{2,1,0:T(8,128)(2,1)S(1)}, bf16[8,80,384]{2,1,0:T(8,128)(2,1)S(1)}, u32[]{:S(2)}, u32[]{:S(2)}) collective-permute-start(bf16[8,80,384]{2,1,0:T(8,128)(2,1)S(1)} %slice.131), channel_id=1, source_target_pairs={{0,8},{8,16},{16,24},{24,0},{1,9},{9,17},{17,25},{25,1},{2,10},{10... | collective-permute-start | bytes 1474568 | tf_op jit(solution)/shard_map/ppermute | solution.py:100
  121.4 1.6 copy-start.3
  125.4 25.5 %all-to-all-start = ((f32[8,64,384]{2,1,0:T(8,128)}), f32[8,64,384]{2,1,0:T(8,128)S(1)}, u32[]{:S(2)}, u32[]{:S(2)}) async-start(f32[8,64,384]{2,1,0:T(8,128)} %fusion.50), calls=%async_computation | async-start | bytes 1572864 | tf_op jit(solution)/shard_map/all_to_all | solution.py:175
  138.7 48.0 %all-gather.5.cloned.1.call-start = ((), (), s32[]{:S(2)}) async-start(), calls=%async_computation.2 | async-start | bytes 2949120 | tf_op jit(solution)/shard_map/all_gather | solution.py:204
  156.4 1.7 copy-start.2
  186.7 5.2 %copy-start.1 = (bf16[4,2,128,256]{3,2,1,0:T(8,128)(2,1)S(1)}, bf16[4,2,128,256]{3,2,1,0:T(8,128)(2,1)}, u32[]{:S(2)}) copy-start(bf16[4,2,128,256]{3,2,1,0:T(8,128)(2,1)} %param.15) | copy-start | bytes 1572868
Sparse Core Ops, SparseCore 0:
  25.3 32.5 all-gather.2
  157.7 28.9 all-gather.4
where the time goes:
time: 200 us; the launch traced here: 199 us
  starting transfers between devices  86.2 us (43%)
  local copies, waits for them, and re-layouts  42.6 us (21%)
  waiting for transfers between devices  34.5 us (17%)
  between operations  17.2 us (9%)
  matrix products  10.5 us (5%)
  other arithmetic  7.76 us (4%)
    ppermute x8, starting transfers between devices, ring_pieces(): behind = lax.ppermute(behind, axis, backward)  41.3 us
    ppermute x8, starting transfers between devices, ring_pieces(): ahead = lax.ppermute(ahead, axis, forward)  17.8 us
    all_to_all x1, starting transfers between devices, shards(): mine = lax.all_to_all(both, 'head', 0, 1, tiled=True)  13.3 us
    ppermute x8, waiting for transfers between devices, ring_pieces(): behind = lax.ppermute(behind, axis, backward)  11.6 us
    all_to_all x1, waiting for transfers between devices, shards(): mine = lax.all_to_all(both, 'head', 0, 1, tiled=True)  10.7 us
    ppermute x2, starting transfers between devices, ring_pieces(): got.append((step, half, lax.ppermute(behind[half:], axis, backward)))  9.89 us
    ppermute x2, waiting for transfers between devices, ring_pieces(): got.append((step, 0, lax.ppermute(ahead[:half], axis, forward)))  9.46 us
    slice x3, local copies, waits for them, and re-layouts, shards(): stacked[:, part_rows:].reshape(tok_count, -1)[:, :wo_flat.shape[0]]  9.38 us
  transfers between devices with their start and end apart: 23, of which 5 were waited for; matrix products, arithmetic and copies ran while one was open for 19% of the time, Pallas kernels for 0%

commit v1 on v0

--- a/solution.py
+++ b/solution.py
@@ -172,7 +172,10 @@
     mean_square = jnp.mean(wide * wide, axis=1, keepdims=True)
     normed = (wide * lax.rsqrt(mean_square + 1e-06)).astype(jnp.bfloat16)
     both = jnp.dot(normed, proj_w, preferred_element_type=jnp.float32)
-    mine = lax.all_to_all(both, "head", 0, 1, tiled=True)
+    mine = jnp.concatenate(
+        lax.all_to_all(jnp.stack(jnp.split(both, lax.axis_size("head"), axis=0)), "head", 0, 0),
+        axis=1,
+    )
     mine = mine.reshape(DRAFT, head_count, q_cols + kv_cols)
     q_pre = mine[:, :, :q_cols].reshape(DRAFT, HQ, HD)
     kv_pre = mine[:, :, q_cols:].reshape(DRAFT, 2 * HD)

time: 200 us -> 210 us (1.050)
  other arithmetic: 7.76 us -> 13.5 us
  local copies, waits for them, and re-layouts: 42.6 us -> 48 us
  waiting for transfers between devices: 34.5 us -> 30.7 us
    slice x3 -> x2, local copies, waits for them, and re-layouts: 9.38 us -> 5.02 us  [shards(): stacked[:, part_rows:].reshape(tok_count, -1)[:, :wo_flat.shape[0]]]
    unnamed x16 -> x59, local copies, waits for them, and re-layouts: 2.81 us -> 7.09 us
    reshape x1 -> x2, local copies, waits for them, and re-layouts: 7.12 us -> 10.9 us  [shards(): wo_cols = stacked[:, part_rows:].reshape(tok_count, -1)[:, :wo_flat.shape...]
    all_to_all x1, waiting for transfers between devices: 10.7 us -> 7.04 us  [shards(): lax.all_to_all(jnp.stack(jnp.split(both, lax.axis_size('head'), axis=0)),...]
    all_gather x1 -> x0, local copies, waits for them, and re-layouts: 2.98 us -> none  [shards(): gathered = lax.all_gather(tokens, 'head', axis=1, tiled=True)]
  transfers between devices with their start and end apart: 23 -> 23, of which waited for: 5 -> 5; matrix products, arithmetic and copies ran while one was open for 19% -> 20% of each run, Pallas kernels for 0% -> 0%
where the time goes in v1:
time: 210 us; the launch traced here: 208 us
  starting transfers between devices  86.2 us (41%)
  local copies, waits for them, and re-layouts  48 us (23%)
  waiting for transfers between devices  30.7 us (15%)
  between operations  17.4 us (8%)
  other arithmetic  13.5 us (6%)
  matrix products  12.5 us (6%)
    ppermute x8, starting transfers between devices, ring_pieces(): behind = lax.ppermute(behind, axis, backward)  41.3 us
    ppermute x8, starting transfers between devices, ring_pieces(): ahead = lax.ppermute(ahead, axis, forward)  17.8 us
    all_to_all x1, starting transfers between devices, shards(): lax.all_to_all(jnp.stack(jnp.split(both, lax.axis_size('head'), axis=0)),...  13.3 us
    ppermute x8, waiting for transfers between devices, ring_pieces(): behind = lax.ppermute(behind, axis, backward)  11.1 us
    reshape x2, local copies, waits for them, and re-layouts, shards(): wo_cols = stacked[:, part_rows:].reshape(tok_count, -1)[:, :wo_flat.shape...  10.9 us
    ppermute x2, starting transfers between devices, ring_pieces(): got.append((step, half, lax.ppermute(behind[half:], axis, backward)))  9.89 us
    ppermute x2, waiting for transfers between devices, ring_pieces(): got.append((step, 0, lax.ppermute(ahead[:half], axis, forward)))  9.45 us
    unnamed x59, local copies, waits for them, and re-layouts  7.09 us
  transfers between devices with their start and end apart: 23, of which 5 were waited for; matrix products, arithmetic and copies ran while one was open for 20% of the time, Pallas kernels for 0%

profile of v1, /device:TPU:1, one launch (start us, length us, event | category | flops | bytes accessed | tf_op | source)
XLA Modules:
  0.0 208.3 jit_solution(17348000472692308198)
XLA Ops:
  7.3 1.2 copy.30
  8.5 1.0 reshape.341
  11.3 4.4 %collective-permute-start = (bf16[80,384]{1,0:T(8,128)(2,1)S(1)}, bf16[80,384]{1,0:T(8,128)(2,1)S(1)}, u32[]{:S(2)}, u32[]{:S(2)}) collective-permute-start(bf16[80,384]{1,0:T(8,128)(2,1)S(1)} %get-tuple-element.6), channel_id=1, source_target_pairs={{0,32},{32,64},{64,96},{96,128},{128,160},{160,192},{192,224},{224... | collective-permute-start | bytes 184328 | tf_op jit(solution)/shard_map/ppermute | solution.py:103
  15.7 9.5 %collective-permute-start.1 = (bf16[80,384]{1,0:T(8,128)(2,1)S(1)}, bf16[80,384]{1,0:T(8,128)(2,1)S(1)}, u32[]{:S(2)}, u32[]{:S(2)}) collective-permute-start(bf16[80,384]{1,0:T(8,128)(2,1)S(1)} %get-tuple-element.6), channel_id=1, source_target_pairs={{0,480},{32,0},{64,32},{96,64},{128,96},{160,128},{192,160},{224,1... | collective-permute-start | bytes 184328 | tf_op jit(solution)/shard_map/ppermute | solution.py:106
  32.7 1.9 collective-permute-start.2
  34.6 4.6 %collective-permute-start.3 = (bf16[80,384]{1,0:T(8,128)(2,1)S(1)}, bf16[80,384]{1,0:T(8,128)(2,1)S(1)}, u32[]{:S(2)}, u32[]{:S(2)}) collective-permute-start(bf16[80,384]{1,0:T(8,128)(2,1)S(1)} %collective-permute-done.1), channel_id=1, source_target_pairs={{0,480},{32,0},{64,32},{96,64},{128,96},{160,128},{192,160},{224,1... | collective-permute-start | bytes 184328 | tf_op jit(solution)/shard_map/ppermute | solution.py:106
  39.3 1.9 collective-permute-start.4
  41.2 4.6 %collective-permute-start.5 = (bf16[80,384]{1,0:T(8,128)(2,1)S(1)}, bf16[80,384]{1,0:T(8,128)(2,1)S(1)}, u32[]{:S(2)}, u32[]{:S(2)}) collective-permute-start(bf16[80,384]{1,0:T(8,128)(2,1)S(1)} %collective-permute-done.3), channel_id=1, source_target_pairs={{0,480},{32,0},{64,32},{96,64},{128,96},{160,128},{192,160},{224,1... | collective-permute-start | bytes 184328 | tf_op jit(solution)/shard_map/ppermute | solution.py:106
  45.8 1.9 collective-permute-start.6
  47.8 4.6 %collective-permute-start.7 = (bf16[80,384]{1,0:T(8,128)(2,1)S(1)}, bf16[80,384]{1,0:T(8,128)(2,1)S(1)}, u32[]{:S(2)}, u32[]{:S(2)}) collective-permute-start(bf16[80,384]{1,0:T(8,128)(2,1)S(1)} %collective-permute-done.5), channel_id=1, source_target_pairs={{0,480},{32,0},{64,32},{96,64},{128,96},{160,128},{192,160},{224,1... | collective-permute-start | bytes 184328 | tf_op jit(solution)/shard_map/ppermute | solution.py:106
  52.4 1.9 collective-permute-start.8
  54.4 4.6 %collective-permute-start.9 = (bf16[80,384]{1,0:T(8,128)(2,1)S(1)}, bf16[80,384]{1,0:T(8,128)(2,1)S(1)}, u32[]{:S(2)}, u32[]{:S(2)}) collective-permute-start(bf16[80,384]{1,0:T(8,128)(2,1)S(1)} %collective-permute-done.7), channel_id=1, source_target_pairs={{0,480},{32,0},{64,32},{96,64},{128,96},{160,128},{192,160},{224,1... | collective-permute-start | bytes 184328 | tf_op jit(solution)/shard_map/ppermute | solution.py:106
  59.0 1.9 collective-permute-start.10
  60.9 4.6 %collective-permute-start.11 = (bf16[80,384]{1,0:T(8,128)(2,1)S(1)}, bf16[80,384]{1,0:T(8,128)(2,1)S(1)}, u32[]{:S(2)}, u32[]{:S(2)}) collective-permute-start(bf16[80,384]{1,0:T(8,128)(2,1)S(1)} %collective-permute-done.9), channel_id=1, source_target_pairs={{0,480},{32,0},{64,32},{96,64},{128,96},{160,128},{192,160},{224,1... | collective-permute-start | bytes 184328 | tf_op jit(solution)/shard_map/ppermute | solution.py:106
  65.6 1.9 collective-permute-start.12
  67.5 4.6 %collective-permute-start.13 = (bf16[80,384]{1,0:T(8,128)(2,1)S(1)}, bf16[80,384]{1,0:T(8,128)(2,1)S(1)}, u32[]{:S(2)}, u32[]{:S(2)}) collective-permute-start(bf16[80,384]{1,0:T(8,128)(2,1)S(1)} %collective-permute-done.11), channel_id=1, source_target_pairs={{0,480},{32,0},{64,32},{96,64},{128,96},{160,128},{192,160},{224,1... | collective-permute-start | bytes 184328 | tf_op jit(solution)/shard_map/ppermute | solution.py:106
  72.2 1.9 collective-permute-start.14
  74.1 4.6 %collective-permute-start.15 = (bf16[40,384]{1,0:T(8,128)(2,1)S(1)}, bf16[40,384]{1,0:T(8,128)(2,1)S(1)}, u32[]{:S(2)}, u32[]{:S(2)}) collective-permute-start(bf16[40,384]{1,0:T(8,128)(2,1)S(1)} %slice.130), channel_id=1, source_target_pairs={{0,480},{32,0},{64,32},{96,64},{128,96},{160,128},{192,160},{224,1... | collective-permute-start | bytes 92168 | tf_op jit(solution)/shard_map/ppermute | solution.py:101
  78.8 0.9 collective-permute-done.15
  79.7 4.4 %collective-permute-start.17 = (bf16[16,80,384]{2,1,0:T(8,128)(2,1)S(1)}, bf16[16,80,384]{2,1,0:T(8,128)(2,1)S(1)}, u32[]{:S(2)}, u32[]{:S(2)}) collective-permute-start(bf16[16,80,384]{2,1,0:T(8,128)(2,1)S(1)} %bitcast_dynamic-update-slice_fusion.20), channel_id=1, source_target_pairs={{0,24},{8,0},{16,8},{24,16},{1,25},{9,1},{17,9},{25,17},{2,26},{10... | collective-permute-start | bytes 2949128 | tf_op jit(solution)/shard_map/ppermute | solution.py:106
  84.1 1.9 collective-permute-start.16
  87.6 11.0 %collective-permute-done.17 = bf16[16,80,384]{2,1,0:T(8,128)(2,1)S(1)} collective-permute-done((bf16[16,80,384]{2,1,0:T(8,128)(2,1)S(1)}, bf16[16,80,384]{2,1,0:T(8,128)(2,1)S(1)}, u32[]{:S(2)}, u32[]{:S(2)}) %collective-permute-start.17) | collective-permute-done | bytes 983072 | tf_op jit(solution)/shard_map/ppermute | solution.py:106
  98.7 5.3 %collective-permute-start.19 = (bf16[8,80,384]{2,1,0:T(8,128)(2,1)S(1)}, bf16[8,80,384]{2,1,0:T(8,128)(2,1)S(1)}, u32[]{:S(2)}, u32[]{:S(2)}) collective-permute-start(bf16[8,80,384]{2,1,0:T(8,128)(2,1)S(1)} %slice.132), channel_id=1, source_target_pairs={{0,24},{8,0},{16,8},{24,16},{1,25},{9,1},{17,9},{25,17},{2,26},{10... | collective-permute-start | bytes 1474568 | tf_op jit(solution)/shard_map/ppermute | solution.py:101
  104.1 1.9 collective-permute-start.18
  106.5 9.5 %collective-permute-done.18 = bf16[8,80,384]{2,1,0:T(8,128)(2,1)S(1)} collective-permute-done((bf16[8,80,384]{2,1,0:T(8,128)(2,1)S(1)}, bf16[8,80,384]{2,1,0:T(8,128)(2,1)S(1)}, u32[]{:S(2)}, u32[]{:S(2)}) %collective-permute-start.18) | collective-permute-done | bytes 491552 | tf_op jit(solution)/shard_map/ppermute | solution.py:100
  116.1 1.7 fusion.55
  117.9 2.5 %fusion = f32[512]{0:T(512)S(1)} fusion(bf16[512,2560]{0,1:T(8,128)(2,1)} %all-gather.3.cloned.1.call-done), kind=kLoop, calls=%fused_computation.4 | loop fusion | flops 3931648 | bytes 2623488 | tf_op jit(solution)/shard_map/reduce_sum | solution.py:172
  120.4 3.1 %fusion.2 = f32[512,384]{1,0:T(8,128)S(1)} fusion(bf16[2560,384]{1,0:T(8,128)(2,1)} %bitcast.165, bf16[512,2560]{0,1:T(8,128)(2,1)S(1)} %copy-done.1, f32[512]{0:T(512)S(1)} %add_rsqrt_fusion), kind=kOutput, calls=%fused_computation.6 | convolution fusion | flops 1010565120 | bytes 5376000 | tf_op jit(solution)/shard_map/dot_general | solution.py:174
  128.7 13.3 %all-to-all-start = ((f32[8,64,384]{2,1,0:T(8,128)}), f32[8,64,384]{2,1,0:T(8,128)S(1)}, u32[]{:S(2)}, u32[]{:S(2)}) async-start(f32[8,64,384]{2,1,0:T(8,128)} %fusion.23), calls=%async_computation | async-start | bytes 1572864 | tf_op jit(solution)/shard_map/all_to_all | solution.py:176
  143.2 1.4 gather_fusion
  144.6 1.2 add_add_fusion
  147.1 7.0 %all-to-all-done = f32[8,64,384]{2,1,0:T(8,128)S(1)} async-done(((f32[8,64,384]{2,1,0:T(8,128)}), f32[8,64,384]{2,1,0:T(8,128)S(1)}, u32[]{:S(2)}, u32[]{:S(2)}) %all-to-all-start) | async-done | bytes 786464 | tf_op jit(solution)/shard_map/all_to_all | solution.py:176
  155.2 0.9 convert.35
  156.7 1.7 convolution_convert_fusion
  158.4 1.3 copy.35
  159.8 1.6 reshape.346
  162.9 1.0 fusion.16
  166.0 1.2 fusion.8
  167.2 3.8 %copy.48 = bf16[64,40,384]{0,2,1:T(8,128)(2,1)} copy(bf16[64,40,384]{2,1,0:T(8,128)(2,1)S(1)} %get-tuple-element.7) | data formatting | bytes 3932160 | tf_op jit(solution)/shard_map/reshape | solution.py:165
  171.0 3.3 %slice.145 = bf16[64,12800]{0,1:T(8,128)(2,1)} slice(bf16[64,15360]{0,1:T(8,128)(2,1)} %bitcast.162), slice={[0:64], [0:12800]} | slice | bytes 3276800 | tf_op jit(solution)/shard_map/slice | solution.py:164
  174.3 7.1 %reshape.352 = bf16[64,2560,5]{0,2,1:T(8,128)(2,1)} reshape(bf16[64,12800]{0,1:T(8,128)(2,1)} %slice.145) | data formatting | bytes 3276800 | tf_op jit(solution)/shard_map/reshape | solution.py:166
  181.5 7.0 %copy.43 = bf16[2560,64,5]{0,2,1:T(8,128)(2,1)S(1)} copy(bf16[2560,64,5]{1,2,0:T(8,128)(2,1)} %bitcast.160) | data formatting | bytes 3276800 | tf_op jit(solution)/shard_map/transpose | solution.py:167
  188.5 3.1 %reshape_reshape.3 = bf16[10,256,320]{1,0,2:T(8,128)(2,1)} reshape(bf16[2560,64,5]{0,2,1:T(8,128)(2,1)S(1)} %copy.43) | data formatting | bytes 3276800 | tf_op jit(solution)/shard_map/reshape;reshape | solution.py:210
  191.6 1.6 gather_fusion.1
  193.2 0.9 broadcast_select_fusion
  194.2 2.2 %all-gather.5.cloned.1.call-done = bf16[10,512,256]{2,1,0:T(8,128)(2,1)} async-done(((bf16[10,64,256]{2,1,0:T(8,128)(2,1)}), bf16[10,512,256]{2,1,0:T(8,128)(2,1)}) %all-gather.5.cloned.1.call-update) | async-done | bytes 2621456 | tf_op jit(solution)/shard_map/all_gather | solution.py:207
  196.3 3.9 %fusion.60 = (bf16[10,512,320]{1,2,0:T(8,128)(2,1)S(1)}, f32[10,512,320]{1,2,0:T(8,128)S(1)}) fusion(bf16[10,512,256]{2,1,0:T(8,128)(2,1)} %all-gather.5.cloned.1.call-done, bf16[10,256,320]{1,0,2:T(8,128)(2,1)} %reshape_reshape.3), kind=kOutput, calls=%fused_computation.149 | convolution fusion | flops 840499200 | bytes 14090240 | tf_op jit(solution)/shard_map/dot_general | solution.py:208
  200.2 1.2 fusion.17
  (157 shorter events, 22.3 us)
Async XLA Ops:
  7.2 136.0 %copy-start = (bf16[4,2,128,256]{3,2,1,0:T(8,128)(2,1)S(1)}, bf16[4,2,128,256]{3,2,1,0:T(8,128)(2,1)}, u32[]{:S(2)}) copy-start(bf16[4,2,128,256]{3,2,1,0:T(8,128)(2,1)} %param.15) | copy-start | bytes 1572868
  7.2 18.2 %copy-start.23 = (s32[8]{0:T(128)S(1)}, s32[8]{0:T(128)}, u32[]{:S(2)}) copy-start(s32[8]{0:T(128)} %param.19) | copy-start | bytes 100
  7.2 20.1 %copy-start.24 = (s32[8]{0:T(128)S(1)}, s32[8]{0:T(128)}, u32[]{:S(2)}) copy-start(s32[8]{0:T(128)} %param.18) | copy-start | bytes 100
  7.2 21.4 %copy-start.16 = (s32[8,4]{0,1:T(4,128)S(1)}, s32[8,4]{0,1:T(4,128)}, u32[]{:S(2)}) copy-start(s32[8,4]{0,1:T(4,128)} %param.16) | copy-start | bytes 388
  7.2 110.6 %all-gather.3.cloned.1.call-start = ((), (), s32[]{:S(2)}) async-start(), calls=%async_computation.1 | async-start | bytes 2949120 | tf_op jit(solution)/shard_map/all_gather | solution.py:170
  11.3 21.3 %collective-permute-start = (bf16[80,384]{1,0:T(8,128)(2,1)S(1)}, bf16[80,384]{1,0:T(8,128)(2,1)S(1)}, u32[]{:S(2)}, u32[]{:S(2)}) collective-permute-start(bf16[80,384]{1,0:T(8,128)(2,1)S(1)} %get-tuple-element.6), channel_id=1, source_target_pairs={{0,32},{32,64},{64,96},{96,128},{128,160},{160,192},{192,224},{224... | collective-permute-start | bytes 184328 | tf_op jit(solution)/shard_map/ppermute | solution.py:103
  15.7 18.9 %collective-permute-start.1 = (bf16[80,384]{1,0:T(8,128)(2,1)S(1)}, bf16[80,384]{1,0:T(8,128)(2,1)S(1)}, u32[]{:S(2)}, u32[]{:S(2)}) collective-permute-start(bf16[80,384]{1,0:T(8,128)(2,1)S(1)} %get-tuple-element.6), channel_id=1, source_target_pairs={{0,480},{32,0},{64,32},{96,64},{128,96},{160,128},{192,160},{224,1... | collective-permute-start | bytes 184328 | tf_op jit(solution)/shard_map/ppermute | solution.py:106
  28.9 3.8 %copy-start.20 = (s32[4]{0:T(128)}, s32[4]{0:T(128)S(1)}, u32[]{:S(2)}) copy-start(s32[4]{0:T(128)S(1)} %select_reduce_fusion) | copy-start | bytes 52
  30.1 57.3 %copy-start.9 = (s32[512]{0:T(512)}, s32[512]{0:T(512)S(1)}, u32[]{:S(2)}) copy-start(s32[512]{0:T(512)S(1)} %iota_subtract_fusion) | copy-start | bytes 6148
  32.7 6.6 %collective-permute-start.2 = (bf16[80,384]{1,0:T(8,128)(2,1)S(1)}, bf16[80,384]{1,0:T(8,128)(2,1)S(1)}, u32[]{:S(2)}, u32[]{:S(2)}) collective-permute-start(bf16[80,384]{1,0:T(8,128)(2,1)S(1)} %collective-permute-done), channel_id=1, source_target_pairs={{0,32},{32,64},{64,96},{96,128},{128,160},{160,192},{192,224},{224... | collective-permute-start | bytes 184328 | tf_op jit(solution)/shard_map/ppermute | solution.py:103
  34.6 6.6 %collective-permute-start.3 = (bf16[80,384]{1,0:T(8,128)(2,1)S(1)}, bf16[80,384]{1,0:T(8,128)(2,1)S(1)}, u32[]{:S(2)}, u32[]{:S(2)}) collective-permute-start(bf16[80,384]{1,0:T(8,128)(2,1)S(1)} %collective-permute-done.1), channel_id=1, source_target_pairs={{0,480},{32,0},{64,32},{96,64},{128,96},{160,128},{192,160},{224,1... | collective-permute-start | bytes 184328 | tf_op jit(solution)/shard_map/ppermute | solution.py:106
  39.3 6.6 %collective-permute-start.4 = (bf16[80,384]{1,0:T(8,128)(2,1)S(1)}, bf16[80,384]{1,0:T(8,128)(2,1)S(1)}, u32[]{:S(2)}, u32[]{:S(2)}) collective-permute-start(bf16[80,384]{1,0:T(8,128)(2,1)S(1)} %collective-permute-done.2), channel_id=1, source_target_pairs={{0,32},{32,64},{64,96},{96,128},{128,160},{160,192},{192,224},{224... | collective-permute-start | bytes 184328 | tf_op jit(solution)/shard_map/ppermute | solution.py:103
  41.2 6.6 %collective-permute-start.5 = (bf16[80,384]{1,0:T(8,128)(2,1)S(1)}, bf16[80,384]{1,0:T(8,128)(2,1)S(1)}, u32[]{:S(2)}, u32[]{:S(2)}) collective-permute-start(bf16[80,384]{1,0:T(8,128)(2,1)S(1)} %collective-permute-done.3), channel_id=1, source_target_pairs={{0,480},{32,0},{64,32},{96,64},{128,96},{160,128},{192,160},{224,1... | collective-permute-start | bytes 184328 | tf_op jit(solution)/shard_map/ppermute | solution.py:106
  45.8 6.6 %collective-permute-start.6 = (bf16[80,384]{1,0:T(8,128)(2,1)S(1)}, bf16[80,384]{1,0:T(8,128)(2,1)S(1)}, u32[]{:S(2)}, u32[]{:S(2)}) collective-permute-start(bf16[80,384]{1,0:T(8,128)(2,1)S(1)} %collective-permute-done.4), channel_id=1, source_target_pairs={{0,32},{32,64},{64,96},{96,128},{128,160},{160,192},{192,224},{224... | collective-permute-start | bytes 184328 | tf_op jit(solution)/shard_map/ppermute | solution.py:103
  47.8 6.6 %collective-permute-start.7 = (bf16[80,384]{1,0:T(8,128)(2,1)S(1)}, bf16[80,384]{1,0:T(8,128)(2,1)S(1)}, u32[]{:S(2)}, u32[]{:S(2)}) collective-permute-start(bf16[80,384]{1,0:T(8,128)(2,1)S(1)} %collective-permute-done.5), channel_id=1, source_target_pairs={{0,480},{32,0},{64,32},{96,64},{128,96},{160,128},{192,160},{224,1... | collective-permute-start | bytes 184328 | tf_op jit(solution)/shard_map/ppermute | solution.py:106
  52.4 6.6 %collective-permute-start.8 = (bf16[80,384]{1,0:T(8,128)(2,1)S(1)}, bf16[80,384]{1,0:T(8,128)(2,1)S(1)}, u32[]{:S(2)}, u32[]{:S(2)}) collective-permute-start(bf16[80,384]{1,0:T(8,128)(2,1)S(1)} %collective-permute-done.6), channel_id=1, source_target_pairs={{0,32},{32,64},{64,96},{96,128},{128,160},{160,192},{192,224},{224... | collective-permute-start | bytes 184328 | tf_op jit(solution)/shard_map/ppermute | solution.py:103
  54.4 6.6 %collective-permute-start.9 = (bf16[80,384]{1,0:T(8,128)(2,1)S(1)}, bf16[80,384]{1,0:T(8,128)(2,1)S(1)}, u32[]{:S(2)}, u32[]{:S(2)}) collective-permute-start(bf16[80,384]{1,0:T(8,128)(2,1)S(1)} %collective-permute-done.7), channel_id=1, source_target_pairs={{0,480},{32,0},{64,32},{96,64},{128,96},{160,128},{192,160},{224,1... | collective-permute-start | bytes 184328 | tf_op jit(solution)/shard_map/ppermute | solution.py:106
  59.0 6.6 %collective-permute-start.10 = (bf16[80,384]{1,0:T(8,128)(2,1)S(1)}, bf16[80,384]{1,0:T(8,128)(2,1)S(1)}, u32[]{:S(2)}, u32[]{:S(2)}) collective-permute-start(bf16[80,384]{1,0:T(8,128)(2,1)S(1)} %collective-permute-done.8), channel_id=1, source_target_pairs={{0,32},{32,64},{64,96},{96,128},{128,160},{160,192},{192,224},{224... | collective-permute-start | bytes 184328 | tf_op jit(solution)/shard_map/ppermute | solution.py:103
  60.9 6.6 %collective-permute-start.11 = (bf16[80,384]{1,0:T(8,128)(2,1)S(1)}, bf16[80,384]{1,0:T(8,128)(2,1)S(1)}, u32[]{:S(2)}, u32[]{:S(2)}) collective-permute-start(bf16[80,384]{1,0:T(8,128)(2,1)S(1)} %collective-permute-done.9), channel_id=1, source_target_pairs={{0,480},{32,0},{64,32},{96,64},{128,96},{160,128},{192,160},{224,1... | collective-permute-start | bytes 184328 | tf_op jit(solution)/shard_map/ppermute | solution.py:106
  65.6 6.6 %collective-permute-start.12 = (bf16[80,384]{1,0:T(8,128)(2,1)S(1)}, bf16[80,384]{1,0:T(8,128)(2,1)S(1)}, u32[]{:S(2)}, u32[]{:S(2)}) collective-permute-start(bf16[80,384]{1,0:T(8,128)(2,1)S(1)} %collective-permute-done.10), channel_id=1, source_target_pairs={{0,32},{32,64},{64,96},{96,128},{128,160},{160,192},{192,224},{224... | collective-permute-start | bytes 184328 | tf_op jit(solution)/shard_map/ppermute | solution.py:103
  67.5 6.6 %collective-permute-start.13 = (bf16[80,384]{1,0:T(8,128)(2,1)S(1)}, bf16[80,384]{1,0:T(8,128)(2,1)S(1)}, u32[]{:S(2)}, u32[]{:S(2)}) collective-permute-start(bf16[80,384]{1,0:T(8,128)(2,1)S(1)} %collective-permute-done.11), channel_id=1, source_target_pairs={{0,480},{32,0},{64,32},{96,64},{128,96},{160,128},{192,160},{224,1... | collective-permute-start | bytes 184328 | tf_op jit(solution)/shard_map/ppermute | solution.py:106
  72.2 6.6 %collective-permute-start.14 = (bf16[40,384]{1,0:T(8,128)(2,1)S(1)}, bf16[40,384]{1,0:T(8,128)(2,1)S(1)}, u32[]{:S(2)}, u32[]{:S(2)}) collective-permute-start(bf16[40,384]{1,0:T(8,128)(2,1)S(1)} %slice.129), channel_id=1, source_target_pairs={{0,32},{32,64},{64,96},{96,128},{128,160},{160,192},{192,224},{224... | collective-permute-start | bytes 92168 | tf_op jit(solution)/shard_map/ppermute | solution.py:100
  74.1 5.6 %collective-permute-start.15 = (bf16[40,384]{1,0:T(8,128)(2,1)S(1)}, bf16[40,384]{1,0:T(8,128)(2,1)S(1)}, u32[]{:S(2)}, u32[]{:S(2)}) collective-permute-start(bf16[40,384]{1,0:T(8,128)(2,1)S(1)} %slice.130), channel_id=1, source_target_pairs={{0,480},{32,0},{64,32},{96,64},{128,96},{160,128},{192,160},{224,1... | collective-permute-start | bytes 92168 | tf_op jit(solution)/shard_map/ppermute | solution.py:101
  79.7 19.0 %collective-permute-start.17 = (bf16[16,80,384]{2,1,0:T(8,128)(2,1)S(1)}, bf16[16,80,384]{2,1,0:T(8,128)(2,1)S(1)}, u32[]{:S(2)}, u32[]{:S(2)}) collective-permute-start(bf16[16,80,384]{2,1,0:T(8,128)(2,1)S(1)} %bitcast_dynamic-update-slice_fusion.20), channel_id=1, source_target_pairs={{0,24},{8,0},{16,8},{24,16},{1,25},{9,1},{17,9},{25,17},{2,26},{10... | collective-permute-start | bytes 2949128 | tf_op jit(solution)/shard_map/ppermute | solution.py:106
  84.1 20.0 %collective-permute-start.16 = (bf16[16,80,384]{2,1,0:T(8,128)(2,1)S(1)}, bf16[16,80,384]{2,1,0:T(8,128)(2,1)S(1)}, u32[]{:S(2)}, u32[]{:S(2)}) collective-permute-start(bf16[16,80,384]{2,1,0:T(8,128)(2,1)S(1)} %bitcast_dynamic-update-slice_fusion.20), channel_id=1, source_target_pairs={{0,8},{8,16},{16,24},{24,0},{1,9},{9,17},{17,25},{25,1},{2,10},{10... | collective-permute-start | bytes 2949128 | tf_op jit(solution)/shard_map/ppermute | solution.py:103
  86.0 1.6 copy-start.11
  86.3 1.4 copy-start.13
  98.7 17.3 %collective-permute-start.19 = (bf16[8,80,384]{2,1,0:T(8,128)(2,1)S(1)}, bf16[8,80,384]{2,1,0:T(8,128)(2,1)S(1)}, u32[]{:S(2)}, u32[]{:S(2)}) collective-permute-start(bf16[8,80,384]{2,1,0:T(8,128)(2,1)S(1)} %slice.132), channel_id=1, source_target_pairs={{0,24},{8,0},{16,8},{24,16},{1,25},{9,1},{17,9},{25,17},{2,26},{10... | collective-permute-start | bytes 1474568 | tf_op jit(solution)/shard_map/ppermute | solution.py:101
  104.1 11.8 %collective-permute-start.18 = (bf16[8,80,384]{2,1,0:T(8,128)(2,1)S(1)}, bf16[8,80,384]{2,1,0:T(8,128)(2,1)S(1)}, u32[]{:S(2)}, u32[]{:S(2)}) collective-permute-start(bf16[8,80,384]{2,1,0:T(8,128)(2,1)S(1)} %slice.131), channel_id=1, source_target_pairs={{0,8},{8,16},{16,24},{24,0},{1,9},{9,17},{17,25},{25,1},{2,10},{10... | collective-permute-start | bytes 1474568 | tf_op jit(solution)/shard_map/ppermute | solution.py:100
  117.9 2.5 %copy-start.1 = (bf16[512,2560]{0,1:T(8,128)(2,1)S(1)}, bf16[512,2560]{0,1:T(8,128)(2,1)}, u32[]{:S(2)}) copy-start(bf16[512,2560]{0,1:T(8,128)(2,1)} %all-gather.3.cloned.1.call-done) | copy-start | bytes 7864324
  128.7 25.5 %all-to-all-start = ((f32[8,64,384]{2,1,0:T(8,128)}), f32[8,64,384]{2,1,0:T(8,128)S(1)}, u32[]{:S(2)}, u32[]{:S(2)}) async-start(f32[8,64,384]{2,1,0:T(8,128)} %fusion.23), calls=%async_computation | async-start | bytes 1572864 | tf_op jit(solution)/shard_map/all_to_all | solution.py:176
  142.0 54.4 %all-gather.5.cloned.1.call-start = ((), (), s32[]{:S(2)}) async-start(), calls=%async_computation.2 | async-start | bytes 2949120 | tf_op jit(solution)/shard_map/all_gather | solution.py:207
  156.1 0.6 copy-start.5
  161.3 0.9 copy-start.4
  161.4 0.9 copy-start.15
  161.4 0.9 copy-start.19
  161.4 1.1 copy-start.10
  161.4 1.1 copy-start.12
  161.4 1.1 copy-start.14
  161.4 1.4 copy-start.2
  161.4 1.4 copy-start.3
  161.4 1.4 copy-start.18
  161.4 1.4 copy-start.22
  162.9 1.3 copy-start.8
  163.8 0.8 copy-start.7
  164.2 1.5 copy-start.6
  166.0 1.2 copy-start.17
  166.0 1.2 copy-start.21
Sparse Core Ops, SparseCore 0:
  25.3 32.5 all-gather.2
  167.3 28.9 all-gather.4
